TPU v7x, 512 devices: a whole 4x4x16 slice. The times are simulated.
512 devices in a mesh: tensor: 32 (over z_hi, x, core), seq: 16 (over z_lo, y).
Axes of the slice: x: 4, y: 4, z: 16 (z_hi: 4, z_lo: 4; z = z_hi * 4 + z_lo), core: 2. Of those that a mesh axis runs over, the one named last changes fastest.
Arguments:
- resid: bfloat16 [16, 512, 2048], P('seq', 'tensor'), may hold values from -6 to 6
- norm_gain: bfloat16 [2048], replicated, may hold values from 0.099609375 to 1.8984375
- gate_weight_matrix: bfloat16 [2048, 10944], P(None, 'tensor'), may hold values from -0.125 to 0.125
- up_weight: bfloat16 [2048, 10944], P(None, 'tensor'), may hold values from -0.125 to 0.125
- w_down: bfloat16 [10944, 2048], P('tensor'), may hold values from -0.0546875 to 0.0546875
- gate_a: bfloat16 [64, 2048, 16], P('seq', 'tensor'), may hold values from -0.125 to 0.125
- gate_b: bfloat16 [64, 16, 10944], P('seq', None, 'tensor'), may hold values from -1.5 to 1.5
- up_a: bfloat16 [64, 2048, 16], P('seq', 'tensor'), may hold values from -0.125 to 0.125
- up_b: bfloat16 [64, 16, 10944], P('seq', None, 'tensor'), may hold values from -1.5 to 1.5
- down_a: bfloat16 [64, 10944, 16], P('seq', 'tensor'), may hold values from -0.0546875 to 0.0546875
- down_b: bfloat16 [64, 16, 2048], P('seq'), may hold values from -1.5 to 1.5
- prompt_lengths: int32 [16, 8], P('seq'), may hold values from 1 to 256, 512 in all within a row
- prompt_choice: int32 [16, 8], P('seq'), may hold values from 0 to 15
- used_adapters: int32 [16], replicated, may hold values from 0 to 63, as said below
- adapter_holder: int32 [64], replicated, may hold values from 0 to 63, each once
Outputs:
- output: bfloat16 [16, 512, 2048], P('seq', 'tensor')
Inputs may be any that keep to these rules, and one draw needn't show every extreme that they name: `used_adapters`: 16 distinct adapter ids.
All inputs are finite; a program needn't handle non-finite values.
Results may differ from a plain program's by a relative error of at most 0.017.
Values may be sent and summed in bfloat16 or wider, within the bound.
No kernel may reach another device: no remote copies, remote signals or barrier semaphores. Data moves between devices by JAX's collectives and lax.ppermute only.
A program may use at most 128 MiB of HBM per device.

v0:
```python
import jax
import jax.numpy as jnp
from jax import lax
from jax.sharding import PartitionSpec as P

adapter_scale = 0.5


def pick_rows(picker, stacked):
    flat = stacked.reshape(stacked.shape[0], -1)
    chosen = jnp.dot(picker, flat, preferred_element_type=jnp.float32).astype(jnp.bfloat16)
    return chosen.reshape((picker.shape[0],) + stacked.shape[1:])


def select_token(values, weights):
    return jnp.sum(values * weights[:, :, None], axis=1)


def local(
    resid,
    norm_gain,
    gate_weight_matrix,
    up_weight,
    w_down,
    gate_a,
    gate_b,
    up_a,
    up_b,
    down_a,
    down_b,
    prompt_lengths,
    prompt_choice,
    used_adapters,
    adapter_holder,
):
    tensor_n = lax.axis_size("tensor")
    tok_dev = resid.shape[1]
    d_model = resid.shape[2]
    group_tok = tok_dev * tensor_n
    used_n = used_adapters.shape[0]
    rank_n = gate_a.shape[2]
    feat_loc = gate_a.shape[1]
    slots_loc = gate_a.shape[0]
    hidden_local = gate_weight_matrix.shape[1]
    adapters_n = adapter_holder.shape[0]
    matches = used_adapters[:, None] == jnp.arange(adapters_n, dtype=jnp.int32)[None, :]
    slot_used = jnp.sum(jnp.where(matches, adapter_holder[None, :], 0), axis=1)
    picker = (slot_used[:, None] == jnp.arange(adapters_n, dtype=jnp.int32)[None, :]).astype(
        jnp.bfloat16
    )
    pieces = (gate_a, up_a, gate_b, up_b, down_a)
    widths = [p.shape[1] * p.shape[2] for p in pieces]
    pack = jnp.concatenate([p.reshape(slots_loc, -1) for p in pieces], axis=1)
    whole = lax.all_gather(pack, "seq", axis=0, tiled=True)
    chosen = pick_rows(picker, whole)
    offs = [0]
    for w in widths:
        offs.append(offs[-1] + w)
    sel = [
        chosen[:, offs[i] : offs[i + 1]].reshape((used_n,) + pieces[i].shape[1:])
        for i in range(len(pieces))
    ]
    sel_ga, sel_ua, sel_gb, sel_ub, sel_da = sel
    whole_db = lax.all_gather(down_b, "seq", axis=0, tiled=True)
    sel_db = pick_rows(picker, whole_db)
    prompt_ends = jnp.cumsum(prompt_lengths[0])
    positions = jnp.arange(group_tok, dtype=jnp.int32)
    prompt_index = jnp.sum((positions[:, None] >= prompt_ends[None, :]).astype(jnp.int32), axis=1)
    prompts_n = prompt_lengths.shape[1]
    hits = prompt_index[:, None] == jnp.arange(prompts_n, dtype=jnp.int32)[None, :]
    tok_choice = jnp.sum(jnp.where(hits, prompt_choice[0][None, :], 0), axis=1)
    token_weights = (tok_choice[:, None] == jnp.arange(used_n, dtype=jnp.int32)[None, :]).astype(
        jnp.float32
    )
    row_first = lax.axis_index("tensor") * tok_dev
    own_weights = lax.dynamic_slice_in_dim(token_weights, row_first, tok_dev, 0)
    residual_float = resid[0].astype(jnp.float32)
    scale = lax.rsqrt(jnp.mean(residual_float * residual_float, axis=-1, keepdims=True) + 1e-06)
    normalized_input = (residual_float * scale * norm_gain.astype(jnp.float32)).astype(jnp.bfloat16)
    tpack = jnp.concatenate(
        [normalized_input.reshape(-1), sel_ga.reshape(-1), sel_ua.reshape(-1)], axis=0
    )
    tall = lax.all_gather(tpack, "tensor", axis=0, tiled=False)
    n_tok_el = tok_dev * d_model
    n_a_el = used_n * feat_loc * rank_n
    piece = tall[:, :n_tok_el].reshape(group_tok, d_model)
    ga_all = tall[:, n_tok_el : n_tok_el + n_a_el].reshape(tensor_n, used_n, feat_loc, rank_n)
    ua_all = tall[:, n_tok_el + n_a_el :].reshape(tensor_n, used_n, feat_loc, rank_n)

    def to_cols(a):
        return jnp.transpose(a, (0, 2, 1, 3)).reshape(tensor_n * feat_loc, used_n * rank_n)

    both_in = jnp.concatenate([to_cols(ga_all), to_cols(ua_all)], axis=1)
    low = jnp.dot(piece, both_in, preferred_element_type=jnp.float32).reshape(
        group_tok, 2, used_n, rank_n
    )
    mid_gate = select_token(low[:, 0], token_weights).astype(jnp.bfloat16)
    mid_up = select_token(low[:, 1], token_weights).astype(jnp.bfloat16)
    weights_bf = token_weights.astype(jnp.bfloat16)

    def spread(mid):
        return (mid[:, None, :] * weights_bf[:, :, None]).reshape(group_tok, used_n * rank_n)

    gate_part = jnp.dot(piece, gate_weight_matrix, preferred_element_type=jnp.float32)
    up_part = jnp.dot(piece, up_weight, preferred_element_type=jnp.float32)
    gate_adapter_rows = jnp.dot(
        spread(mid_gate),
        sel_gb.reshape(used_n * rank_n, hidden_local),
        preferred_element_type=jnp.float32,
    )
    up_adapter_rows = jnp.dot(
        spread(mid_up),
        sel_ub.reshape(used_n * rank_n, hidden_local),
        preferred_element_type=jnp.float32,
    )
    gate_preactivation = gate_part + adapter_scale * gate_adapter_rows
    up_preactivation = up_part + adapter_scale * up_adapter_rows
    hidden = (jax.nn.silu(gate_preactivation) * up_preactivation).astype(jnp.bfloat16)
    down_part = jnp.dot(hidden, w_down, preferred_element_type=jnp.float32).astype(jnp.bfloat16)
    da_cols = jnp.transpose(sel_da, (1, 0, 2)).reshape(hidden_local, used_n * rank_n)
    down_adapter_rows = jnp.dot(hidden, da_cols, preferred_element_type=jnp.float32).reshape(
        group_tok, used_n, rank_n
    )
    partial_down = select_token(down_adapter_rows, token_weights).astype(jnp.bfloat16)
    joined = jnp.concatenate([down_part, partial_down], axis=1)
    reduced = lax.psum_scatter(joined, "tensor", scatter_dimension=0, tiled=True)
    down_total_sum = reduced[:, :d_model].astype(jnp.float32)
    mid_down = reduced[:, d_model:]
    spread_down = (mid_down[:, None, :] * own_weights.astype(jnp.bfloat16)[:, :, None]).reshape(
        tok_dev, used_n * rank_n
    )
    adapter_down_term = jnp.dot(
        spread_down,
        sel_db.reshape(used_n * rank_n, sel_db.shape[2]),
        preferred_element_type=jnp.float32,
    )
    return (residual_float + down_total_sum + adapter_scale * adapter_down_term).astype(
        jnp.bfloat16
    )[None]


def solution(mesh):
    placed = (
        P("seq", "tensor", None),
        P(),
        P(None, "tensor"),
        P(None, "tensor"),
        P("tensor", None),
        P("seq", "tensor", None),
        P("seq", None, "tensor"),
        P("seq", "tensor", None),
        P("seq", None, "tensor"),
        P("seq", "tensor", None),
        P("seq", None, None),
        P("seq", None),
        P("seq", None),
        P(),
        P(),
    )
    return jax.shard_map(
        local, mesh=mesh, in_specs=placed, out_specs=P("seq", "tensor", None), check_vma=False
    )
```

profile of v0, /device:TPU:8, one launch (start us, length us, event | category | flops | bytes accessed | tf_op | source)
XLA Modules:
  0.0 427.2 jit_solution(15833528576533599783)
XLA Ops:
  6.6 1.1 copy.47
  7.7 0.3 reshape.179
  8.0 0.8 copy.45
  8.8 0.1 reshape.175
  8.9 0.8 copy.46
  9.7 0.1 reshape.176
  9.9 0.9 reshape.177
  10.8 0.9 reshape.178
  11.7 0.9 concatenate.12
  12.7 0.7 convert_element_type.82
  13.5 0.1 fusion.18
  13.8 0.2 select_reduce_fusion.1
  14.0 91.6 %all-gather.10.cloned.1.call-done = bf16[16,4,18464]{2,1,0:T(4,128)(2,1)} async-done(((bf16[1,4,18464]{2,1,0:T(4,128)(2,1)}), bf16[16,4,18464]{2,1,0:T(4,128)(2,1)}) %all-gather.10.cloned.1.call-update) | async-done | bytes 2363408 | tf_op jit(solution)/shard_map/all_gather | solution.py:54
  105.6 4.3 %reshape.194 = bf16[64,18464]{1,0:T(8,128)(2,1)} reshape(bf16[16,4,18464]{2,1,0:T(4,128)(2,1)} %all-gather.10.cloned.1.call-done) | data formatting | bytes 4726784
  110.0 2.2 convolution_convert_fusion.1
  112.2 0.7 pad_maximum_fusion.2
  112.9 0.7 all-gather.6.cloned.1.call-update
  113.7 0.2 reduce-window.8
  113.8 0.1 convert_reduce_fusion
  113.9 0.1 select_reduce_fusion
  114.0 0.2 fusion.24
  114.2 1.0 reshape_reshape.17
  115.2 1.0 reshape_reshape.18
  116.2 1.0 reshape.187
  117.2 1.2 copy.52
  118.4 87.7 %all-gather.8.cloned.1.call-done = bf16[2097152]{0:T(1024)(128)(2,1)} async-done(((bf16[65536]{0:T(1024)(128)(2,1)}), bf16[2097152]{0:T(1024)(128)(2,1)}) %all-gather.8.cloned.1.call-update) | async-done | bytes 4194320 | tf_op jit(solution)/shard_map/all_gather | solution.py:83
  206.2 5.5 %reshape.192 = bf16[32,65536]{1,0:T(8,128)(2,1)} reshape(bf16[2097152]{0:T(1024)(128)(2,1)} %all-gather.8.cloned.1.call-done) | data formatting | bytes 8388608 | tf_op jit(solution)/shard_map/all_gather | solution.py:83
  211.7 1.7 slice.50
  213.4 2.4 reshape.195
  215.8 2.4 reshape.180
  218.2 2.7 fusion.23
  221.0 3.1 copy.48
  224.1 4.9 %copy.49 = bf16[32,64,16,16]{1,0,3,2:T(8,128)(2,1)S(1)} copy(bf16[32,64,16,16]{0,3,1,2:T(8,128)(2,1)} %bitcast.93) | data formatting | bytes 2097152 | tf_op jit(solution)/shard_map/transpose | solution.py:91
  228.9 2.4 reshape.182
  231.4 4.6 %copy.50 = bf16[32,16384]{0,1:T(8,128)(2,1)} copy(bf16[32,16384]{1,0:T(8,128)(2,1)} %get-tuple-element.8) | data formatting | bytes 2097152 | tf_op jit(solution)/shard_map/slice | solution.py:88
  236.0 4.9 %copy.51 = bf16[32,64,16,16]{1,0,3,2:T(8,128)(2,1)S(1)} copy(bf16[32,64,16,16]{0,3,1,2:T(8,128)(2,1)} %bitcast.94) | data formatting | bytes 2097152 | tf_op jit(solution)/shard_map/transpose | solution.py:91
  240.8 2.4 reshape.184
  243.3 2.0 pad_maximum_fusion.1
  245.3 0.3 copy-done.2
  245.6 1.3 fusion.3
  246.9 0.1 fusion.13
  247.0 0.1 copy-done.1
  247.2 0.4 copy-done.10
  247.6 0.9 fusion.25
  248.5 0.3 fusion.7
  248.8 0.2 copy-done.11
  249.0 0.9 fusion.26
  250.0 0.4 fusion.8
  250.4 0.5 copy-done.5
  250.9 0.3 fusion.9
  251.2 0.1 copy.53
  251.3 1.3 convolution_convert_fusion.2
  252.6 1.6 pad_maximum_fusion
  254.2 0.1 dynamic-slice_convert_fusion
  254.3 0.1 copy.54
  254.4 40.6 %all-gather.6.cloned.1.call-done = bf16[64,16,2048]{2,1,0:T(8,128)(2,1)} async-done(((bf16[4,16,2048]{2,1,0:T(8,128)(2,1)}), bf16[64,16,2048]{2,1,0:T(8,128)(2,1)}) %all-gather.6.cloned.1.call-update) | async-done | bytes 4194320 | tf_op jit(solution)/shard_map/all_gather | solution.py:64
  295.0 4.6 %copy.61 = bf16[8,8,16,2048]{3,1,2,0:T(8,128)(2,1)S(1)} copy(bf16[8,8,16,2048]{3,2,1,0:T(8,128)(2,1)} %bitcast.97) | data formatting | bytes 8388608
  299.7 0.7 convolution_convert_fusion
  300.4 0.5 reshape_reshape.19
  300.9 117.1 %reduce-scatter.2.cloned.1.call-done = bf16[16,2064]{1,0:T(8,128)(2,1)} async-done(((bf16[512,2064]{1,0:T(8,128)(2,1)}), bf16[16,2064]{1,0:T(8,128)(2,1)}) %reduce-scatter.2.cloned.1.call-update) | async-done | bytes 66064 | tf_op jit(solution)/shard_map/reduce_scatter | solution.py:126
  418.1 0.7 slice.59
  418.7 0.1 broadcast_multiply_fusion.2
  418.8 0.1 mul.160
  419.0 1.8 fusion.2
  (45 shorter events, 0.5 us)
Async XLA Ops:
  6.5 244.8 %copy-start = (bf16[342,2048]{1,0:T(8,128)(2,1)S(1)}, bf16[342,2048]{1,0:T(8,128)(2,1)}, u32[]{:S(2)}) copy-start(bf16[342,2048]{1,0:T(8,128)(2,1)} %param.19) | copy-start | bytes 4202500
  6.5 6.9 %copy-start.4 = (bf16[1,16,2048]{2,1,0:T(8,128)(2,1)S(1)}, bf16[1,16,2048]{2,1,0:T(8,128)(2,1)}, u32[]{:S(2)}) copy-start(bf16[1,16,2048]{2,1,0:T(8,128)(2,1)} %param.15) | copy-start | bytes 196612
  6.5 7.3 %copy-start.13 = (s32[16]{0:T(128)S(1)}, s32[16]{0:T(128)}, u32[]{:S(2)}) copy-start(s32[16]{0:T(128)} %param.28) | copy-start | bytes 196
  6.5 7.3 %copy-start.12 = (s32[64]{0:T(128)S(1)}, s32[64]{0:T(128)}, u32[]{:S(2)}) copy-start(s32[64]{0:T(128)} %param.29) | copy-start | bytes 772
  6.5 99.1 %all-gather.10.cloned.1.call-start = ((), (), s32[]{:S(2)}) async-start(), calls=%async_computation.4 | async-start | bytes 2524160 | tf_op jit(solution)/shard_map/all_gather | solution.py:54
  12.7 193.5 %all-gather.8.cloned.1.call-start = ((), (), s32[]{:S(2)}) async-start(), calls=%async_computation.3 | async-start | bytes 4325376 | tf_op jit(solution)/shard_map/all_gather | solution.py:83
  14.0 95.9 %copy-start.7 = (s32[16]{0:T(128)}, s32[16]{0:T(128)S(1)}, u32[]{:S(2)}) copy-start(s32[16]{0:T(128)S(1)} %select_reduce_fusion.1) | copy-start | bytes 196
  109.9 3.7 copy-start.14
  109.9 4.0 copy-start.9
  112.9 182.2 %all-gather.6.cloned.1.call-start = ((), (), s32[]{:S(2)}) async-start(), calls=%async_computation.2 | async-start | bytes 4456448 | tf_op jit(solution)/shard_map/all_gather | solution.py:64
  113.6 304.4 %reduce-scatter.2.cloned.1.call-start = ((), (), s32[]{:S(2)}) async-start(), calls=%async_computation.1 | async-start | bytes 2297856 | tf_op jit(solution)/shard_map/reduce_scatter | solution.py:126
  243.3 2.3 copy-start.2
  245.6 1.6 copy-start.1
  245.6 2.0 copy-start.10
  247.5 0.9 copy-start.3
  247.5 1.5 copy-start.11
  249.0 0.9 copy-start.6
  250.0 0.9 copy-start.5
  295.0 4.6 %copy-start.8 = (s32[16]{0:T(128)S(1)}, s32[16]{0:T(128)}, u32[]{:S(2)}) copy-start(s32[16]{0:T(128)} %copy-done.7) | copy-start | bytes 196
Sparse Core Ops, SparseCore 0:
  12.8 92.7 all-gather.9
  113.0 93.1 all-gather.7
  208.3 86.7 all-gather.5
  299.5 118.5 reduce-scatter.1
where the time goes:
time: 428 us; the launch traced here: 427 us
  waiting for transfers between devices  338 us (79%)
  local copies, waits for them, and re-layouts  59.9 us (14%)
  between operations  13.5 us (3%)
  matrix products  10 us (2%)
  other arithmetic  5.86 us (1%)
    reduce_scatter x1, waiting for transfers between devices, local(): lax.psum_scatter(joined, 'tensor', scatter_dimension=0, tiled=True)  117 us
    all_gather x1, waiting for transfers between devices, local(): whole = lax.all_gather(pack, 'seq', axis=0, tiled=True)  91.6 us
    all_gather x1, waiting for transfers between devices, local(): tall = lax.all_gather(tpack, 'tensor', axis=0, tiled=False)  87.7 us
    all_gather x1, waiting for transfers between devices, local(): whole_db = lax.all_gather(down_b, 'seq', axis=0, tiled=True)  40.6 us
    unnamed x43, local copies, waits for them, and re-layouts  13.5 us
    transpose x2, local copies, waits for them, and re-layouts, to_cols(): jnp.transpose(a, (0, 2, 1, 3)).reshape(tensor_n * feat_loc, used_n * rank_n)  9.76 us
  transfers between devices with their start and end apart: 4, of which 4 were waited for; matrix products, arithmetic and copies ran while one was open for 14% of the time, Pallas kernels for 0%

commit v1 on v0

--- a/solution.py
+++ b/solution.py
@@ -51,7 +51,9 @@
     pieces = (gate_a, up_a, gate_b, up_b, down_a)
     widths = [p.shape[1] * p.shape[2] for p in pieces]
     pack = jnp.concatenate([p.reshape(slots_loc, -1) for p in pieces], axis=1)
-    whole = lax.all_gather(pack, "seq", axis=0, tiled=True)
+    whole = jnp.concatenate(
+        lax.all_to_all(jnp.stack([pack] * lax.axis_size("seq")), "seq", 0, 0), axis=0
+    )
     chosen = pick_rows(picker, whole)
     offs = [0]
     for w in widths:

time: 428 us -> 402 us (0.939)
  waiting for transfers between devices: 338 us -> 301 us
  starting transfers between devices: 0.15 us -> 10.2 us
    all_gather x1 -> x0, waiting for transfers between devices: 91.6 us -> none  [local(): whole = lax.all_gather(pack, 'seq', axis=0, tiled=True)]
    all_to_all x0 -> x1, waiting for transfers between devices: none -> 44.7 us  [local(): lax.all_to_all(jnp.stack([pack] * lax.axis_size('seq')), 'seq', 0, 0)]
    all_gather x1, waiting for transfers between devices: 87.7 us -> 98 us  [local(): tall = lax.all_gather(tpack, 'tensor', axis=0, tiled=False)]
    all_to_all x0 -> x1, starting transfers between devices: none -> 10.1 us  [local(): lax.all_to_all(jnp.stack([pack] * lax.axis_size('seq')), 'seq', 0, 0)]
    reshape x0 -> x1, local copies, waits for them, and re-layouts: none -> 4.34 us  [local(): jnp.concatenate(lax.all_to_all(jnp.stack([pack] * lax.axis_size('seq')),...]
    unnamed x43 -> x44, local copies, waits for them, and re-layouts: 13.5 us -> 9.2 us
where the time goes in v1:
time: 402 us; the launch traced here: 401 us
  waiting for transfers between devices  301 us (75%)
  local copies, waits for them, and re-layouts  61.3 us (15%)
  between operations  13.5 us (3%)
  starting transfers between devices  10.2 us (3%)
  matrix products  10 us (2%)
  other arithmetic  5.17 us (1%)
    reduce_scatter x1, waiting for transfers between devices, local(): lax.psum_scatter(joined, 'tensor', scatter_dimension=0, tiled=True)  117 us
    all_gather x1, waiting for transfers between devices, local(): tall = lax.all_gather(tpack, 'tensor', axis=0, tiled=False)  98 us
    all_to_all x1, waiting for transfers between devices, local(): lax.all_to_all(jnp.stack([pack] * lax.axis_size('seq')), 'seq', 0, 0)  44.7 us
    all_gather x1, waiting for transfers between devices, local(): whole_db = lax.all_gather(down_b, 'seq', axis=0, tiled=True)  40.5 us
    all_to_all x1, starting transfers between devices, local(): lax.all_to_all(jnp.stack([pack] * lax.axis_size('seq')), 'seq', 0, 0)  10.1 us
    transpose x2, local copies, waits for them, and re-layouts, to_cols(): jnp.transpose(a, (0, 2, 1, 3)).reshape(tensor_n * feat_loc, used_n * rank_n)  9.76 us
    unnamed x44, local copies, waits for them, and re-layouts  9.2 us
  transfers between devices with their start and end apart: 4, of which 4 were waited for; matrix products, arithmetic and copies ran while one was open for 14% of the time, Pallas kernels for 0%

profile of v1, /device:TPU:8, one launch (start us, length us, event | category | flops | bytes accessed | tf_op | source)
XLA Modules:
  0.0 401.4 jit_solution(9721921179251261117)
XLA Ops:
  6.5 1.1 copy.47
  7.7 0.3 reshape.184
  7.9 0.8 copy.45
  8.7 0.1 reshape.180
  8.9 0.8 copy.46
  9.7 0.1 reshape.181
  9.8 0.9 reshape.182
  10.7 0.9 reshape.183
  11.7 0.3 concatenate.12
  12.0 2.0 stack.2
  14.0 10.1 %all-to-all-start = ((bf16[16,4,18464]{2,1,0:T(4,128)(2,1)}), bf16[16,4,18464]{2,1,0:T(4,128)(2,1)}, u32[]{:S(2)}, u32[]{:S(2)}) async-start(bf16[16,4,18464]{2,1,0:T(4,128)(2,1)} %stack.2), calls=%async_computation | async-start | bytes 4751360 | tf_op jit(solution)/shard_map/all_to_all | solution.py:55
  24.3 0.1 fusion.18
  24.6 0.2 select_reduce_fusion.1
  24.8 44.7 %all-to-all-done = bf16[16,4,18464]{2,1,0:T(4,128)(2,1)} async-done(((bf16[16,4,18464]{2,1,0:T(4,128)(2,1)}), bf16[16,4,18464]{2,1,0:T(4,128)(2,1)}, u32[]{:S(2)}, u32[]{:S(2)}) %all-to-all-start) | async-done | bytes 2363424 | tf_op jit(solution)/shard_map/all_to_all | solution.py:55
  69.6 4.3 %reshape.185 = bf16[64,18464]{1,0:T(8,128)(2,1)} reshape(bf16[16,4,18464]{2,1,0:T(4,128)(2,1)} %all-to-all-done) | data formatting | bytes 4726784 | tf_op jit(solution)/shard_map/reshape | solution.py:54
  73.9 2.2 convolution_convert_fusion.1
  76.1 0.7 pad_maximum_fusion.2
  76.9 0.7 all-gather.4.cloned.1.call-update
  77.6 0.2 reduce-window.8
  77.8 0.1 convert_reduce_fusion
  77.9 0.1 select_reduce_fusion
  78.0 0.2 fusion.24
  78.2 1.0 reshape_reshape.17
  79.1 1.0 reshape_reshape.18
  80.1 1.0 reshape.193
  81.2 1.2 copy.52
  82.4 98.0 %all-gather.6.cloned.1.call-done = bf16[2097152]{0:T(1024)(128)(2,1)} async-done(((bf16[65536]{0:T(1024)(128)(2,1)}), bf16[2097152]{0:T(1024)(128)(2,1)}) %all-gather.6.cloned.1.call-update) | async-done | bytes 4194320 | tf_op jit(solution)/shard_map/all_gather | solution.py:85
  180.4 5.5 %reshape.198 = bf16[32,65536]{1,0:T(8,128)(2,1)} reshape(bf16[2097152]{0:T(1024)(128)(2,1)} %all-gather.6.cloned.1.call-done) | data formatting | bytes 8388608 | tf_op jit(solution)/shard_map/all_gather | solution.py:85
  185.9 1.7 slice.50
  187.6 2.4 reshape.199
  190.0 2.4 reshape.186
  192.4 2.7 fusion.23
  195.2 3.1 copy.48
  198.3 4.9 %copy.49 = bf16[32,64,16,16]{1,0,3,2:T(8,128)(2,1)S(1)} copy(bf16[32,64,16,16]{0,3,1,2:T(8,128)(2,1)} %bitcast.92) | data formatting | bytes 2097152 | tf_op jit(solution)/shard_map/transpose | solution.py:93
  203.2 2.4 reshape.188
  205.6 4.6 %copy.50 = bf16[32,16384]{0,1:T(8,128)(2,1)} copy(bf16[32,16384]{1,0:T(8,128)(2,1)} %get-tuple-element.8) | data formatting | bytes 2097152 | tf_op jit(solution)/shard_map/slice | solution.py:90
  210.2 4.9 %copy.51 = bf16[32,64,16,16]{1,0,3,2:T(8,128)(2,1)S(1)} copy(bf16[32,64,16,16]{0,3,1,2:T(8,128)(2,1)} %bitcast.93) | data formatting | bytes 2097152 | tf_op jit(solution)/shard_map/transpose | solution.py:93
  215.1 2.4 reshape.190
  217.5 2.0 pad_maximum_fusion.1
  219.5 0.3 copy-done.2
  219.8 1.3 fusion.3
  221.1 0.1 fusion.13
  221.2 0.1 copy-done.1
  221.4 0.4 copy-done.11
  221.8 0.9 fusion.25
  222.7 0.3 fusion.7
  223.0 0.2 copy-done.12
  223.3 0.9 fusion.26
  224.2 0.4 fusion.8
  224.6 0.5 copy-done.5
  225.1 0.3 fusion.9
  225.4 0.1 copy.53
  225.6 1.3 convolution_convert_fusion.2
  226.9 1.6 pad_maximum_fusion
  228.5 0.1 copy.54
  228.6 40.5 %all-gather.4.cloned.1.call-done = bf16[64,16,2048]{2,1,0:T(8,128)(2,1)} async-done(((bf16[4,16,2048]{2,1,0:T(8,128)(2,1)}), bf16[64,16,2048]{2,1,0:T(8,128)(2,1)}) %all-gather.4.cloned.1.call-update) | async-done | bytes 4194320 | tf_op jit(solution)/shard_map/all_gather | solution.py:66
  269.1 4.6 %copy.61 = bf16[8,8,16,2048]{3,1,2,0:T(8,128)(2,1)S(1)} copy(bf16[8,8,16,2048]{3,2,1,0:T(8,128)(2,1)} %bitcast.96) | data formatting | bytes 8388608
  273.8 0.7 convolution_convert_fusion
  274.5 0.5 reshape_reshape.19
  275.0 117.1 %reduce-scatter.2.cloned.1.call-done = bf16[16,2064]{1,0:T(8,128)(2,1)} async-done(((bf16[512,2064]{1,0:T(8,128)(2,1)}), bf16[16,2064]{1,0:T(8,128)(2,1)}) %reduce-scatter.2.cloned.1.call-update) | async-done | bytes 66064 | tf_op jit(solution)/shard_map/reduce_scatter | solution.py:128
  392.2 0.7 slice.59
  392.8 0.1 broadcast_multiply_fusion.2
  392.9 0.1 mul.160
  393.1 1.8 fusion.2
  (47 shorter events, 0.6 us)
Async XLA Ops:
  6.5 219.0 %copy-start = (bf16[342,2048]{1,0:T(8,128)(2,1)S(1)}, bf16[342,2048]{1,0:T(8,128)(2,1)}, u32[]{:S(2)}) copy-start(bf16[342,2048]{1,0:T(8,128)(2,1)} %param.19) | copy-start | bytes 4202500
  14.0 10.2 %copy-start.7 = (bf16[2048]{0:T(1024)(128)(2,1)S(1)}, bf16[2048]{0:T(1024)(128)(2,1)}, u32[]{:S(2)}) copy-start(bf16[2048]{0:T(1024)(128)(2,1)} %param.16) | copy-start | bytes 12292
  14.0 10.2 %copy-start.4 = (bf16[1,16,2048]{2,1,0:T(8,128)(2,1)S(1)}, bf16[1,16,2048]{2,1,0:T(8,128)(2,1)}, u32[]{:S(2)}) copy-start(bf16[1,16,2048]{2,1,0:T(8,128)(2,1)} %param.15) | copy-start | bytes 196612
  14.0 10.6 %copy-start.13 = (s32[64]{0:T(128)S(1)}, s32[64]{0:T(128)}, u32[]{:S(2)}) copy-start(s32[64]{0:T(128)} %param.29) | copy-start | bytes 772
  14.0 10.6 %copy-start.14 = (s32[16]{0:T(128)S(1)}, s32[16]{0:T(128)}, u32[]{:S(2)}) copy-start(s32[16]{0:T(128)} %param.28) | copy-start | bytes 196
  14.0 55.5 %all-to-all-start = ((bf16[16,4,18464]{2,1,0:T(4,128)(2,1)}), bf16[16,4,18464]{2,1,0:T(4,128)(2,1)}, u32[]{:S(2)}, u32[]{:S(2)}) async-start(bf16[16,4,18464]{2,1,0:T(4,128)(2,1)} %stack.2), calls=%async_computation | async-start | bytes 4751360 | tf_op jit(solution)/shard_map/all_to_all | solution.py:55
  24.1 156.3 %all-gather.6.cloned.1.call-start = ((), (), s32[]{:S(2)}) async-start(), calls=%async_computation.4 | async-start | bytes 4325376 | tf_op jit(solution)/shard_map/all_gather | solution.py:85
  24.8 49.1 %copy-start.8 = (s32[16]{0:T(128)}, s32[16]{0:T(128)S(1)}, u32[]{:S(2)}) copy-start(s32[16]{0:T(128)S(1)} %select_reduce_fusion.1) | copy-start | bytes 196
  73.9 3.7 copy-start.15
  73.9 4.0 copy-start.10
  76.8 192.3 %all-gather.4.cloned.1.call-start = ((), (), s32[]{:S(2)}) async-start(), calls=%async_computation.3 | async-start | bytes 4456448 | tf_op jit(solution)/shard_map/all_gather | solution.py:66
  77.6 314.6 %reduce-scatter.2.cloned.1.call-start = ((), (), s32[]{:S(2)}) async-start(), calls=%async_computation.2 | async-start | bytes 2297856 | tf_op jit(solution)/shard_map/reduce_scatter | solution.py:128
  217.5 2.3 copy-start.2
  219.8 1.6 copy-start.1
  219.8 2.0 copy-start.11
  221.8 0.9 copy-start.3
  221.8 1.5 copy-start.12
  223.3 0.9 copy-start.6
  224.2 0.9 copy-start.5
  269.1 4.6 %copy-start.9 = (s32[16]{0:T(128)S(1)}, s32[16]{0:T(128)}, u32[]{:S(2)}) copy-start(s32[16]{0:T(128)} %copy-done.8) | copy-start | bytes 196
Sparse Core Ops, SparseCore 0:
  76.9 103.4 all-gather.5
  182.5 86.6 all-gather.3
  273.7 118.3 reduce-scatter.1
